TPU v7x, 32 devices: a whole 2x2x4 slice. The times are simulated.
32 devices in a mesh: row: 8 (over z, y), rep: 4 (over x, core).
Axes of the slice: x: 2, y: 2, z: 4, core: 2. Of those that a mesh axis runs over, the one named last changes fastest.
Arguments:
- features: bfloat16 [2048, 256], P('row'), may hold values from -6 to 6
- cotangent: bfloat16 [2048, 256], P('row'), may hold values from -0.3125 to 0.3125
- weight_one: bfloat16 [256, 256], replicated, may hold values from -0.375 to 0.375
- weight_two: bfloat16 [256, 256], replicated, may hold values from -0.375 to 0.375
- block_index: int32 [8, 4, 2, 4], P('row', 'rep'), may hold values from 0 to 15, as said below
- block_count: int32 [8, 4, 2], P('row', 'rep'), may hold values from 0 to 4
- block_values: bfloat16 [8, 4, 2, 4, 128, 128], P('row', 'rep'), as said below
Outputs:
- logits: bfloat16 [2048, 256], P(('row', 'rep'))
- grad_one: float32 [256, 256], replicated
- grad_two: float32 [256, 256], replicated
Inputs may be any that keep to these rules, and one draw needn't show every extreme that they name: block_index[i, j, a, s] lies in [j * 4, (j + 1) * 4); for s < block_count[i, j, a] the entries rise strictly; later entries equal j * 4 and are not part of A. `block_values`: A is symmetric: block (r, c) is listed exactly when block (c, r) is, and its entries are the transpose of those of block (c, r). Entries are normal with standard deviation (0.5 * 128 * 16) ** -0.5, cut at five such deviations; blocks on the diagonal are symmetric.
All inputs are finite; a program needn't handle non-finite values.
Results may differ from a plain program's by a relative error of at most 0.0059.
Values may be sent and summed in bfloat16 or wider, within the bound.
No kernel may reach another device: no remote copies, remote signals or barrier semaphores. Data moves between devices by JAX's collectives and lax.ppermute only.
A program may use at most 64 MiB of HBM per device.

v0:
```python
import jax
import jax.numpy as jnp
from jax import lax
from jax.sharding import PartitionSpec as P


def broadcast(array, axis, root):
    mine = lax.axis_index(axis) == root
    return lax.psum(jnp.where(mine, array, jnp.zeros_like(array)), axis)


def aggregate(source, block_index, block_count, block_values):
    copies = lax.axis_size("rep")
    sections = lax.axis_size("row") // copies
    copy_index = lax.axis_index("rep")
    node_rows, feature_width = source.shape
    block_rows = block_values.shape[2]
    slot_count = block_values.shape[3]
    block_side = block_values.shape[-1]

    def fetch(state_unused, section_index):
        panel = broadcast(source, "row", copy_index * sections + section_index)
        return (state_unused, panel)

    state_unused, panels = lax.scan(fetch, jnp.int32(0), jnp.arange(sections, dtype=jnp.int32))
    panels = panels.reshape(sections * block_rows, block_side, feature_width)
    columns = block_index[0, 0] - copy_index * slot_count
    live_slots = jnp.arange(slot_count, dtype=jnp.int32)[None, :] < block_count[0, 0][:, None]
    picked = jnp.take(panels, columns.reshape(-1), axis=0).reshape(
        block_rows, slot_count, block_side, feature_width
    )
    picked = jnp.where(live_slots[:, :, None, None], picked, jnp.zeros((), picked.dtype))
    partial_value = lax.dot_general(
        block_values[0, 0],
        picked,
        (((1, 3), (1, 2)), ((0,), (0,))),
        preferred_element_type=jnp.float32,
    )
    partial_value = partial_value.reshape(node_rows, feature_width)
    result = lax.psum(partial_value, "rep")
    return result


def shards(features, cotangent, weight_one, weight_two, block_index, block_count, block_values):
    copies = lax.axis_size("rep")
    copy_index = lax.axis_index("rep")
    node_rows = features.shape[0]
    share_rows = node_rows // copies
    first_row = copy_index * share_rows

    def own_rows(array):
        return lax.dynamic_slice_in_dim(array, first_row, share_rows, 0)

    agg_one = aggregate(features, block_index, block_count, block_values).astype(jnp.bfloat16)
    pre_one = jnp.dot(agg_one, weight_one, preferred_element_type=jnp.float32)
    hidden = jax.nn.silu(pre_one).astype(jnp.bfloat16)
    agg_two = aggregate(hidden, block_index, block_count, block_values).astype(jnp.bfloat16)
    agg_two_own = own_rows(agg_two)
    logits = jnp.dot(agg_two_own, weight_two, preferred_element_type=jnp.float32).astype(
        jnp.bfloat16
    )
    cotangent_own = own_rows(cotangent)
    grad_two = lax.dot_general(
        agg_two_own, cotangent_own, (((0,), (0,)), ((), ())), preferred_element_type=jnp.float32
    )
    grad_two = lax.psum(grad_two, ("row", "rep"))
    back_signal = lax.dot_general(
        cotangent, weight_two, (((1,), (1,)), ((), ())), preferred_element_type=jnp.float32
    ).astype(jnp.bfloat16)
    carried = aggregate(back_signal, block_index, block_count, block_values)
    carried = own_rows(carried)
    pre_own = own_rows(pre_one)
    agg_one_own = own_rows(agg_one)
    gate_value = jax.nn.sigmoid(pre_own)
    pre_grad = (carried * (gate_value + pre_own * gate_value * (1.0 - gate_value))).astype(
        jnp.bfloat16
    )
    grad_one = lax.dot_general(
        agg_one_own, pre_grad, (((0,), (0,)), ((), ())), preferred_element_type=jnp.float32
    )
    grad_one = lax.psum(grad_one, ("row", "rep"))
    return (logits, grad_one, grad_two)


def solution(mesh):
    in_specs = (
        P("row", None),
        P("row", None),
        P(),
        P(),
        P("row", "rep", None, None),
        P("row", "rep", None),
        P("row", "rep", None, None, None, None),
    )
    out_specs = (P(("row", "rep"), None), P(), P())
    return jax.shard_map(shards, mesh=mesh, in_specs=in_specs, out_specs=out_specs, check_vma=False)
```

profile of v0, /device:TPU:0, one launch (start us, length us, event | category | flops | bytes accessed | tf_op | source)
XLA Modules:
  0.0 661.8 jit_solution(11847135036822304722)
XLA Ops:
  8.0 0.7 copy-done.4
  8.9 1.2 convolution_convert_fusion
  10.1 154.0 %while.38 = (s32[]{:T(128)}, bf16[2,256,256]{2,1,0:T(8,128)(2,1)S(1)}, s32[2]{0:T(128)S(1)}, s32[]{:T(128)}, bf16[256,256]{1,0:T(8,128)(2,1)S(1)}, /*index=5*/s32[]{:T(128)}, u32[]{:T(128)}, u32[]{:T(128)}) while((s32[]{:T(128)}, bf16[2,256,256]{2,1,0:T(8,128)(2,1)S(1)}, s32[2]{0:T(128)S(1)}, s32[]{:T(128)}, ...), condition=%wide.region_10.12_spmd, body=%wide.region_8.11_spmd.sunk | while | flops 131079 | bytes 1310923 | solution.py:25
  12.1 75.9 %all-reduce.17.cloned.1.call-done = bf16[1,256,256]{2,1,0:T(8,128)(2,1)} async-done(((bf16[1,256,256]{2,1,0:T(8,128)(2,1)}), bf16[1,256,256]{2,1,0:T(8,128)(2,1)}) %all-reduce.17.cloned.1.call-update) | async-done | bytes 131088 | tf_op jit(solution)/shard_map/while/body/eval_jaxpr/psum | solution.py:9
  88.0 0.9 constant_dynamic-update-slice_fusion.8
  90.9 72.3 %all-reduce.17.cloned.1.call-done = bf16[1,256,256]{2,1,0:T(8,128)(2,1)} async-done(((bf16[1,256,256]{2,1,0:T(8,128)(2,1)}), bf16[1,256,256]{2,1,0:T(8,128)(2,1)}) %all-reduce.17.cloned.1.call-update) | async-done | bytes 131088 | tf_op jit(solution)/shard_map/while/body/eval_jaxpr/psum | solution.py:9
  163.2 0.9 constant_dynamic-update-slice_fusion.8
  164.7 0.9 copy-done.1
  165.6 150.0 %while.36 = (s32[]{:T(128)}, bf16[2,256,256]{2,1,0:T(8,128)(2,1)S(1)}, s32[2]{0:T(128)S(1)}, s32[]{:T(128)}, bf16[256,256]{1,0:T(8,128)(2,1)S(1)}, /*index=5*/s32[]{:T(128)}, u32[]{:T(128)}, u32[]{:T(128)}) while((s32[]{:T(128)}, bf16[2,256,256]{2,1,0:T(8,128)(2,1)S(1)}, s32[2]{0:T(128)S(1)}, s32[]{:T(128)}, bf16[256,256]{1,0:T(8,128)(2,1)S(1)}, ...), condition=%wide.region_2.3_spmd, body=%wide.region_0.2_spmd.sunk | while | flops 131079 | bytes 1310923 | solution.py:25
  166.8 0.7 select_bitcast_fusion.6
  167.5 72.3 %all-reduce.13.cloned.1.call-done = bf16[1,256,256]{2,1,0:T(8,128)(2,1)} async-done(((bf16[1,256,256]{2,1,0:T(8,128)(2,1)}), bf16[1,256,256]{2,1,0:T(8,128)(2,1)}) %all-reduce.13.cloned.1.call-update) | async-done | bytes 131088 | tf_op jit(solution)/shard_map/while/body/eval_jaxpr/psum | solution.py:9
  239.8 0.9 constant_dynamic-update-slice_fusion.6
  242.8 71.9 %all-reduce.13.cloned.1.call-done = bf16[1,256,256]{2,1,0:T(8,128)(2,1)} async-done(((bf16[1,256,256]{2,1,0:T(8,128)(2,1)}), bf16[1,256,256]{2,1,0:T(8,128)(2,1)}) %all-reduce.13.cloned.1.call-update) | async-done | bytes 131088 | tf_op jit(solution)/shard_map/while/body/eval_jaxpr/psum | solution.py:9
  314.7 0.9 constant_dynamic-update-slice_fusion.6
  317.4 13.1 %all-reduce.18 = bf16[256,256]{1,0:T(8,128)(2,1)S(1)} all-reduce(f32[256,256]{1,0:T(8,128)S(1)} %bitcast.65), channel_id=1, replica_groups=mesh['row'=8,'rep'=4] {'rep'}, use_global_device_ids=true, to_apply=%region_3.5 | all-reduce | flops 65536 | bytes 393216 | tf_op jit(solution)/shard_map/psum | solution.py:40
  330.5 1.0 fusion
  331.8 150.5 %while.37 = (s32[]{:T(128)}, bf16[2,256,256]{2,1,0:T(8,128)(2,1)S(1)}, s32[2]{0:T(128)S(1)}, s32[]{:T(128)}, bf16[256,256]{1,0:T(8,128)(2,1)S(1)}, /*index=5*/s32[]{:T(128)}, u32[]{:T(128)}, u32[]{:T(128)}) while((s32[]{:T(128)}, bf16[2,256,256]{2,1,0:T(8,128)(2,1)S(1)}, s32[2]{0:T(128)S(1)}, s32[]{:T(128)}, bf16[256,256]{1,0:T(8,128)(2,1)S(1)}, ...), condition=%wide.region_6.8_spmd, body=%wide.region_4.7_spmd.sunk | while | flops 131079 | bytes 1310923 | solution.py:25
  333.1 0.7 select_bitcast_fusion.7
  333.8 72.7 %all-reduce.15.cloned.1.call-done = bf16[1,256,256]{2,1,0:T(8,128)(2,1)} async-done(((bf16[1,256,256]{2,1,0:T(8,128)(2,1)}), bf16[1,256,256]{2,1,0:T(8,128)(2,1)}) %all-reduce.15.cloned.1.call-update) | async-done | bytes 131088 | tf_op jit(solution)/shard_map/while/body/eval_jaxpr/psum | solution.py:9
  406.5 0.9 constant_dynamic-update-slice_fusion.7
  408.8 0.7 select_bitcast_fusion.7
  409.5 71.9 %all-reduce.15.cloned.1.call-done = bf16[1,256,256]{2,1,0:T(8,128)(2,1)} async-done(((bf16[1,256,256]{2,1,0:T(8,128)(2,1)}), bf16[1,256,256]{2,1,0:T(8,128)(2,1)}) %all-reduce.15.cloned.1.call-update) | async-done | bytes 131088 | tf_op jit(solution)/shard_map/while/body/eval_jaxpr/psum | solution.py:9
  481.4 0.9 constant_dynamic-update-slice_fusion.7
  484.0 13.8 %all-reduce.19 = bf16[256,256]{1,0:T(8,128)(2,1)S(1)} all-reduce(f32[256,256]{1,0:T(8,128)S(1)} %bitcast.64), channel_id=1, replica_groups=mesh['row'=8,'rep'=4] {'rep'}, use_global_device_ids=true, to_apply=%region_7.9 | all-reduce | flops 65536 | bytes 393216 | tf_op jit(solution)/shard_map/psum | solution.py:40
  497.7 1.7 fusion.16
  499.4 17.9 %all-reduce.9.cloned.1.call-done = f32[256,256]{1,0:T(8,128)} async-done(((f32[256,256]{1,0:T(8,128)}), f32[256,256]{1,0:T(8,128)}) %all-reduce.9.cloned.1.call-update) | async-done | bytes 262160 | tf_op jit(solution)/shard_map/psum | solution.py:40
  517.3 1.8 fusion.15
  519.1 0.9 copy-done.2
  519.9 0.8 convolution_convert_fusion.1
  520.7 131.2 %all-reduce.11.cloned.1.call-done = (f32[256,256]{1,0:T(8,128)}, f32[256,256]{1,0:T(8,128)}) async-done(((f32[256,256]{1,0:T(8,128)}, f32[256,256]{1,0:T(8,128)}), (f32[256,256]{1,0:T(8,128)}, f32[256,256]{1,0:T(8,128)})) %all-reduce.11.cloned.1.call-update) | async-done | bytes 524304 | tf_op jit(solution)/shard_map/psum | solution.py:81
  651.9 1.7 copy.44
  653.6 0.7 copy.45
  (56 shorter events, 10.2 us)
Async XLA Ops:
  8.0 309.1 %copy-start = (bf16[1,1,2,4,128,128]{5,4,3,2,1,0:T(8,128)(2,1)S(1)}, bf16[1,1,2,4,128,128]{5,4,3,2,1,0:T(8,128)(2,1)}, u32[]{:S(2)}) copy-start(bf16[1,1,2,4,128,128]{5,4,3,2,1,0:T(8,128)(2,1)} %param.21) | copy-start | bytes 786436
  8.0 0.7 copy-start.4
  10.1 77.9 %all-reduce.17.cloned.1.call-start = ((), (), s32[]{:S(2)}) async-start(), calls=%async_computation.4 | async-start | bytes 262144 | tf_op jit(solution)/shard_map/while/body/eval_jaxpr/psum | solution.py:9
  88.9 74.3 %all-reduce.17.cloned.1.call-start = ((), (), s32[]{:S(2)}) async-start(), calls=%async_computation.4 | async-start | bytes 262144 | tf_op jit(solution)/shard_map/while/body/eval_jaxpr/psum | solution.py:9
  164.7 0.9 copy-start.1
  165.6 74.2 %all-reduce.13.cloned.1.call-start = ((), (), s32[]{:S(2)}) async-start(), calls=%async_computation.2 | async-start | bytes 262144 | tf_op jit(solution)/shard_map/while/body/eval_jaxpr/psum | solution.py:9
  240.8 73.9 %all-reduce.13.cloned.1.call-start = ((), (), s32[]{:S(2)}) async-start(), calls=%async_computation.2 | async-start | bytes 262144 | tf_op jit(solution)/shard_map/while/body/eval_jaxpr/psum | solution.py:9
  316.2 0.7 copy-start.6
  330.5 1.0 copy-start.5
  331.8 74.7 %all-reduce.15.cloned.1.call-start = ((), (), s32[]{:S(2)}) async-start(), calls=%async_computation.3 | async-start | bytes 262144 | tf_op jit(solution)/shard_map/while/body/eval_jaxpr/psum | solution.py:9
  407.5 73.9 %all-reduce.15.cloned.1.call-start = ((), (), s32[]{:S(2)}) async-start(), calls=%async_computation.3 | async-start | bytes 262144 | tf_op jit(solution)/shard_map/while/body/eval_jaxpr/psum | solution.py:9
  482.3 35.0 %all-reduce.9.cloned.1.call-start = ((), (), s32[]{:S(2)}) async-start(), calls=%async_computation | async-start | bytes 524288 | tf_op jit(solution)/shard_map/psum | solution.py:40
  482.9 169.0 %all-reduce.11.cloned.1.call-start = ((), (), s32[]{:S(2)}) async-start(), calls=%async_computation.1 | async-start | bytes 1048576 | tf_op jit(solution)/shard_map/psum | solution.py:81
  519.0 0.9 copy-start.2
  651.9 1.7 copy-start.3
Sparse Core Ops, SparseCore 0:
  14.8 73.1 all-reduce.16
  93.6 69.4 all-reduce.16
  170.3 69.4 all-reduce.12
  245.2 69.4 all-reduce.12
  336.2 70.2 all-reduce.14
  411.9 69.4 all-reduce.14
Sparse Core Ops, SparseCore 1:
  485.7 31.5 all-reduce.8
  523.2 128.7 all-reduce.10
where the time goes:
time: 662 us
  waiting for transfers between devices  587 us (89%)
  blocking collectives  26.8 us (4%)
  local copies, waits for them, and re-layouts  16.4 us (2%)
  between operations  15.7 us (2%)
  matrix products  7.22 us (1%)
    psum x6, waiting for transfers between devices, broadcast(): return lax.psum(jnp.where(mine, array, jnp.zeros_like(array)), axis)  437 us
    psum x1, waiting for transfers between devices, shards(): grad_one = lax.psum(grad_one, ('row', 'rep'))  131 us
    psum x2, blocking collectives, aggregate(): result = lax.psum(partial_value, 'rep')  26.8 us
    psum x1, waiting for transfers between devices, aggregate(): result = lax.psum(partial_value, 'rep')  17.9 us
  transfers between devices with their start and end apart: 8, of which 8 were waited for; matrix products, arithmetic and copies ran while one was open for 1% of the time, Pallas kernels for 0%

commit v1 on v0

--- a/solution.py
+++ b/solution.py
@@ -37,7 +37,9 @@
         preferred_element_type=jnp.float32,
     )
     partial_value = partial_value.reshape(node_rows, feature_width)
-    result = lax.psum(partial_value, "rep")
+    result = partial_value
+    for hop in (1, 2):
+        result = result + lax.ppermute(result, "rep", [(dev, dev ^ hop) for dev in range(4)])
     return result
 
 

time: 662 us -> 633 us (0.956)
  blocking collectives: 26.8 us -> 0 us
    psum x2 -> x0, blocking collectives: 26.8 us -> none  [aggregate(): result = lax.psum(partial_value, 'rep')]
    ppermute x0 -> x6, waiting for transfers between devices: none -> 18.4 us  [aggregate(): lax.ppermute(result, 'rep', [(dev, dev ^ hop) for dev in range(4)])]
    psum x1 -> x0, waiting for transfers between devices: 17.9 us -> none  [aggregate(): result = lax.psum(partial_value, 'rep')]
  transfers between devices with their start and end apart: 8 -> 13, of which waited for: 8 -> 11; matrix products, arithmetic and copies ran while one was open for 1% -> 1% of each run, Pallas kernels for 0% -> 0%
where the time goes in v1:
time: 633 us
  waiting for transfers between devices  581 us (92%)
  local copies, waits for them, and re-layouts  16.4 us (3%)
  between operations  15.7 us (2%)
    psum x6, waiting for transfers between devices, broadcast(): return lax.psum(jnp.where(mine, array, jnp.zeros_like(array)), axis)  436 us
    psum x1, waiting for transfers between devices, shards(): grad_one = lax.psum(grad_one, ('row', 'rep'))  126 us
    ppermute x6, waiting for transfers between devices, aggregate(): lax.ppermute(result, 'rep', [(dev, dev ^ hop) for dev in range(4)])  18.4 us
  transfers between devices with their start and end apart: 13, of which 11 were waited for; matrix products, arithmetic and copies ran while one was open for 1% of the time, Pallas kernels for 0%

profile of v1, /device:TPU:0, one launch (start us, length us, event | category | flops | bytes accessed | tf_op | source)
XLA Modules:
  0.0 632.6 jit_solution(7113601868899990367)
XLA Ops:
  8.0 0.7 copy-done.4
  8.9 1.2 convolution_convert_fusion
  10.1 154.0 %while.38 = (s32[]{:T(128)}, bf16[2,256,256]{2,1,0:T(8,128)(2,1)S(1)}, s32[2]{0:T(128)S(1)}, s32[]{:T(128)}, bf16[256,256]{1,0:T(8,128)(2,1)S(1)}, /*index=5*/s32[]{:T(128)}, u32[]{:T(128)}, u32[]{:T(128)}) while((s32[]{:T(128)}, bf16[2,256,256]{2,1,0:T(8,128)(2,1)S(1)}, s32[2]{0:T(128)S(1)}, s32[]{:T(128)}, bf16[256,256]{1,0:T(8,128)(2,1)S(1)}, ...), condition=%wide.region_8.10_spmd, body=%wide.region_6.9_spmd.sunk | while | flops 131079 | bytes 1310923 | solution.py:25
  12.1 75.9 %all-reduce.12.cloned.1.call-done = bf16[1,256,256]{2,1,0:T(8,128)(2,1)} async-done(((bf16[1,256,256]{2,1,0:T(8,128)(2,1)}), bf16[1,256,256]{2,1,0:T(8,128)(2,1)}) %all-reduce.12.cloned.1.call-update) | async-done | bytes 131088 | tf_op jit(solution)/shard_map/while/body/eval_jaxpr/psum | solution.py:9
  88.0 0.9 constant_dynamic-update-slice_fusion.8
  90.9 72.3 %all-reduce.12.cloned.1.call-done = bf16[1,256,256]{2,1,0:T(8,128)(2,1)} async-done(((bf16[1,256,256]{2,1,0:T(8,128)(2,1)}), bf16[1,256,256]{2,1,0:T(8,128)(2,1)}) %all-reduce.12.cloned.1.call-update) | async-done | bytes 131088 | tf_op jit(solution)/shard_map/while/body/eval_jaxpr/psum | solution.py:9
  163.2 0.9 constant_dynamic-update-slice_fusion.8
  164.7 0.9 copy-done.1
  165.6 150.0 %while.36 = (s32[]{:T(128)}, bf16[2,256,256]{2,1,0:T(8,128)(2,1)S(1)}, s32[2]{0:T(128)S(1)}, s32[]{:T(128)}, bf16[256,256]{1,0:T(8,128)(2,1)S(1)}, /*index=5*/s32[]{:T(128)}, u32[]{:T(128)}, u32[]{:T(128)}) while((s32[]{:T(128)}, bf16[2,256,256]{2,1,0:T(8,128)(2,1)S(1)}, s32[2]{0:T(128)S(1)}, s32[]{:T(128)}, bf16[256,256]{1,0:T(8,128)(2,1)S(1)}, ...), condition=%wide.region_2.3_spmd, body=%wide.region_0.2_spmd.sunk | while | flops 131079 | bytes 1310923 | solution.py:25
  167.5 72.3 %all-reduce.8.cloned.1.call-done = bf16[1,256,256]{2,1,0:T(8,128)(2,1)} async-done(((bf16[1,256,256]{2,1,0:T(8,128)(2,1)}), bf16[1,256,256]{2,1,0:T(8,128)(2,1)}) %all-reduce.8.cloned.1.call-update) | async-done | bytes 131088 | tf_op jit(solution)/shard_map/while/body/eval_jaxpr/psum | solution.py:9
  239.8 0.9 constant_dynamic-update-slice_fusion.6
  242.8 71.9 %all-reduce.8.cloned.1.call-done = bf16[1,256,256]{2,1,0:T(8,128)(2,1)} async-done(((bf16[1,256,256]{2,1,0:T(8,128)(2,1)}), bf16[1,256,256]{2,1,0:T(8,128)(2,1)}) %all-reduce.8.cloned.1.call-update) | async-done | bytes 131088 | tf_op jit(solution)/shard_map/while/body/eval_jaxpr/psum | solution.py:9
  314.7 0.9 constant_dynamic-update-slice_fusion.6
  317.5 1.5 collective-permute-done
  319.1 1.5 collective-permute-start.1
  321.0 6.5 %collective-permute-done.1 = f32[256,256]{1,0:T(8,128)S(1)} collective-permute-done((f32[256,256]{1,0:T(8,128)S(1)}, f32[256,256]{1,0:T(8,128)S(1)}, u32[]{:S(2)}, u32[]{:S(2)}) %collective-permute-start.1) | collective-permute-done | bytes 262176 | tf_op jit(solution)/shard_map/ppermute | solution.py:42
  327.8 149.8 %while.37 = (s32[]{:T(128)}, bf16[2,256,256]{2,1,0:T(8,128)(2,1)S(1)}, s32[2]{0:T(128)S(1)}, s32[]{:T(128)}, bf16[256,256]{1,0:T(8,128)(2,1)S(1)}, /*index=5*/s32[]{:T(128)}, u32[]{:T(128)}, u32[]{:T(128)}) while((s32[]{:T(128)}, bf16[2,256,256]{2,1,0:T(8,128)(2,1)S(1)}, s32[2]{0:T(128)S(1)}, s32[]{:T(128)}, bf16[256,256]{1,0:T(8,128)(2,1)S(1)}, ...), condition=%wide.region_5.7_spmd, body=%wide.region_3.6_spmd.sunk | while | flops 131079 | bytes 1310923 | solution.py:25
  329.8 72.0 %all-reduce.10.cloned.1.call-done = bf16[1,256,256]{2,1,0:T(8,128)(2,1)} async-done(((bf16[1,256,256]{2,1,0:T(8,128)(2,1)}), bf16[1,256,256]{2,1,0:T(8,128)(2,1)}) %all-reduce.10.cloned.1.call-update) | async-done | bytes 131088 | tf_op jit(solution)/shard_map/while/body/eval_jaxpr/psum | solution.py:9
  401.8 0.9 constant_dynamic-update-slice_fusion.7
  404.7 71.9 %all-reduce.10.cloned.1.call-done = bf16[1,256,256]{2,1,0:T(8,128)(2,1)} async-done(((bf16[1,256,256]{2,1,0:T(8,128)(2,1)}), bf16[1,256,256]{2,1,0:T(8,128)(2,1)}) %all-reduce.10.cloned.1.call-update) | async-done | bytes 131088 | tf_op jit(solution)/shard_map/while/body/eval_jaxpr/psum | solution.py:9
  476.7 0.9 constant_dynamic-update-slice_fusion.7
  478.8 1.5 collective-permute-start.5
  480.4 1.5 collective-permute-start.3
  481.8 6.2 collective-permute-done.5
  488.0 0.9 fusion.18
  489.0 4.2 collective-permute-done.3
  493.2 1.7 fusion.20
  494.9 0.9 copy-done.2
  495.8 0.8 convolution_convert_fusion.1
  496.5 126.2 %all-reduce.6.cloned.1.call-done = (f32[256,256]{1,0:T(8,128)}, f32[256,256]{1,0:T(8,128)}) async-done(((f32[256,256]{1,0:T(8,128)}, f32[256,256]{1,0:T(8,128)}), (f32[256,256]{1,0:T(8,128)}, f32[256,256]{1,0:T(8,128)})) %all-reduce.6.cloned.1.call-update) | async-done | bytes 524304 | tf_op jit(solution)/shard_map/psum | solution.py:83
  622.8 1.7 copy.39
  624.5 0.7 copy.40
  (68 shorter events, 12.3 us)
Async XLA Ops:
  8.0 309.1 %copy-start = (bf16[1,1,2,4,128,128]{5,4,3,2,1,0:T(8,128)(2,1)S(1)}, bf16[1,1,2,4,128,128]{5,4,3,2,1,0:T(8,128)(2,1)}, u32[]{:S(2)}) copy-start(bf16[1,1,2,4,128,128]{5,4,3,2,1,0:T(8,128)(2,1)} %param.21) | copy-start | bytes 786436
  8.0 0.7 copy-start.4
  10.1 77.9 %all-reduce.12.cloned.1.call-start = ((), (), s32[]{:S(2)}) async-start(), calls=%async_computation.3 | async-start | bytes 262144 | tf_op jit(solution)/shard_map/while/body/eval_jaxpr/psum | solution.py:9
  88.9 74.3 %all-reduce.12.cloned.1.call-start = ((), (), s32[]{:S(2)}) async-start(), calls=%async_computation.3 | async-start | bytes 262144 | tf_op jit(solution)/shard_map/while/body/eval_jaxpr/psum | solution.py:9
  164.7 0.9 copy-start.1
  165.6 74.2 %all-reduce.8.cloned.1.call-start = ((), (), s32[]{:S(2)}) async-start(), calls=%async_computation.1 | async-start | bytes 262144 | tf_op jit(solution)/shard_map/while/body/eval_jaxpr/psum | solution.py:9
  240.8 73.9 %all-reduce.8.cloned.1.call-start = ((), (), s32[]{:S(2)}) async-start(), calls=%async_computation.1 | async-start | bytes 262144 | tf_op jit(solution)/shard_map/while/body/eval_jaxpr/psum | solution.py:9
  316.2 0.7 copy-start.6
  317.4 1.6 collective-permute-start
  319.1 8.4 %collective-permute-start.1 = (f32[256,256]{1,0:T(8,128)S(1)}, f32[256,256]{1,0:T(8,128)S(1)}, u32[]{:S(2)}, u32[]{:S(2)}) collective-permute-start(f32[256,256]{1,0:T(8,128)S(1)} %bitcast_add_fusion.2), channel_id=1, source_target_pairs={{0,2},{1,3},{2,0},{3,1},{4,6},{5,7},{6,4},{7,5},{8,10},{9,11},{10,... | collective-permute-start | bytes 786440 | tf_op jit(solution)/shard_map/ppermute | solution.py:42
  320.9 157.8 %collective-permute-start.4 = (f32[256,256]{1,0:T(8,128)S(1)}, f32[256,256]{1,0:T(8,128)S(1)}, u32[]{:S(2)}, u32[]{:S(2)}) collective-permute-start(f32[256,256]{1,0:T(8,128)S(1)} %bitcast.69), channel_id=1, source_target_pairs={{0,1},{1,0},{2,3},{3,2},{4,5},{5,4},{6,7},{7,6},{8,9},{9,8},{10,11... | collective-permute-start | bytes 786440 | tf_op jit(solution)/shard_map/ppermute | solution.py:42
  321.0 6.5 %copy-start.5 = (bf16[256,256]{1,0:T(8,128)(2,1)S(1)}, bf16[256,256]{1,0:T(8,128)(2,1)}, u32[]{:S(2)}) copy-start(bf16[256,256]{1,0:T(8,128)(2,1)} %param.17) | copy-start | bytes 393220
  327.8 74.0 %all-reduce.10.cloned.1.call-start = ((), (), s32[]{:S(2)}) async-start(), calls=%async_computation.2 | async-start | bytes 262144 | tf_op jit(solution)/shard_map/while/body/eval_jaxpr/psum | solution.py:9
  402.7 73.9 %all-reduce.10.cloned.1.call-start = ((), (), s32[]{:S(2)}) async-start(), calls=%async_computation.2 | async-start | bytes 262144 | tf_op jit(solution)/shard_map/while/body/eval_jaxpr/psum | solution.py:9
  477.6 145.2 %all-reduce.6.cloned.1.call-start = ((), (), s32[]{:S(2)}) async-start(), calls=%async_computation | async-start | bytes 1048576 | tf_op jit(solution)/shard_map/psum | solution.py:83
  478.7 1.7 collective-permute-start.2
  478.8 9.2 %collective-permute-start.5 = (f32[256,256]{1,0:T(8,128)S(1)}, f32[256,256]{1,0:T(8,128)S(1)}, u32[]{:S(2)}, u32[]{:S(2)}) collective-permute-start(f32[256,256]{1,0:T(8,128)S(1)} %bitcast_add_fusion), channel_id=1, source_target_pairs={{0,2},{1,3},{2,0},{3,1},{4,6},{5,7},{6,4},{7,5},{8,10},{9,11},{10,... | collective-permute-start | bytes 786440 | tf_op jit(solution)/shard_map/ppermute | solution.py:42
  480.4 12.8 %collective-permute-start.3 = (f32[256,256]{1,0:T(8,128)S(1)}, f32[256,256]{1,0:T(8,128)S(1)}, u32[]{:S(2)}, u32[]{:S(2)}) collective-permute-start(f32[256,256]{1,0:T(8,128)S(1)} %bitcast_add_fusion.1), channel_id=1, source_target_pairs={{0,2},{1,3},{2,0},{3,1},{4,6},{5,7},{6,4},{7,5},{8,10},{9,11},{10,... | collective-permute-start | bytes 786440 | tf_op jit(solution)/shard_map/ppermute | solution.py:42
  494.9 0.9 copy-start.2
  622.8 1.7 copy-start.3
Sparse Core Ops, SparseCore 0:
  14.8 73.1 all-reduce.11
  93.6 69.4 all-reduce.11
  170.3 69.4 all-reduce.7
  245.2 69.4 all-reduce.7
  332.2 69.5 all-reduce.9
  407.1 69.4 all-reduce.9
Sparse Core Ops, SparseCore 1:
  495.0 127.7 all-reduce.5
